TPU v7x, 256 devices: a whole 4x4x8 slice. The times are simulated.
256 devices in a mesh: own: 32 (over x, z), row: 8 (over y, core).
Axes of the slice: x: 4, y: 4, z: 8, core: 2. Of those that a mesh axis runs over, the one named last changes fastest.
Arguments:
- sigma_anc: float32 [16384, 16384], P('row', 'own'), may hold values from -1.5 to 1.5
- row_blocks: int32 [64, 8], replicated, may hold values from 0 to 63, as said below
- panel1: float32 [64, 2048, 256], P('own', 'row'), may hold values from -0.375 to 0.375
- diag_inv1: float32 [64, 256, 256], P('own'), as said below
- mask1: int32 [64, 8], P('own', 'row'), may hold values 0 or 1
- parent_block2: float32 [64, 256, 256], P('own'), may hold values from -0.375 to 0.375
- panel2: float32 [64, 2048, 256], P('own', 'row'), may hold values from -0.375 to 0.375
- diag_inv2: float32 [64, 256, 256], P('own'), as said below
- mask2: int32 [64, 8], P('own', 'row'), may hold values 0 or 1
Outputs:
- sel1_panel: float32 [64, 2048, 256], P('own', 'row')
- sel1_diag: float32 [64, 256, 256], P('own')
- sel2_parent: float32 [64, 256, 256], P('own')
- sel2_panel: float32 [64, 2048, 256], P('own', 'row')
- sel2_diag: float32 [64, 256, 256], P('own')
Inputs may be any that keep to these rules, and one draw needn't show every extreme that they name: `row_blocks`: entry l of each row lies in block rows 8 * l to 8 * (l + 1) - 1; for supernodes s with the same s // 2, the entries of one column l lie in different aligned runs of 2 block rows. `diag_inv1`: lower triangular, with diagonal entries from 1 to 2. `diag_inv2`: lower triangular, with diagonal entries from 1 to 2.
All inputs are finite; a program needn't handle non-finite values. No bound on the sum of `mask1` or of `mask2` on one device may be relied on, other than what follows from the above.
Results may differ from a plain program's by a relative error of at most 0.000071.
Values sent between devices are 32-bit elements; how exact they have to be, the bound alone decides.
No kernel may reach another device: no remote copies, remote signals or barrier semaphores. Data moves between devices by JAX's collectives and lax.ppermute only.
A program may use at most 128 MiB of HBM per device.

v0:
```python
import jax
import jax.numpy as jnp
from jax import lax
from jax.sharding import PartitionSpec as P

B = 256
HIGH = lax.Precision.HIGHEST


def shifted(shard, axis, by):
    length = lax.axis_size(axis)
    return lax.ppermute(shard, axis, [(i, (i + by) % length) for i in range(length)])


def product(form, left, right):
    return jnp.einsum(form, left, right, precision=HIGH)


def select_send(sigma_local, row_blocks, slots):
    own_count = lax.axis_size("own")
    own_here = lax.axis_index("own")
    row_here = lax.axis_index("row")
    rows_here = sigma_local.shape[0] // B
    cols_here = sigma_local.shape[1] // B
    rowlist = row_blocks.reshape(own_count, slots, -1)
    group = own_here * cols_here // rows_here
    want_col = lax.dynamic_index_in_dim(rowlist, group, 2, keepdims=False)
    local_col = want_col - own_here * cols_here
    match = ((local_col >= 0) & (local_col < cols_here)).astype(jnp.int32)
    which = jnp.sum(match * jnp.arange(slots, dtype=jnp.int32)[None, :], axis=1)
    chosen = rowlist[jnp.arange(own_count, dtype=jnp.int32), which]
    chosen_row = (
        lax.dynamic_index_in_dim(chosen, row_here, 1, keepdims=False) - row_here * rows_here
    )
    chosen_col = jnp.clip(
        lax.dynamic_index_in_dim(chosen, group, 1, keepdims=False) - own_here * cols_here,
        0,
        cols_here - 1,
    )
    blocks4 = sigma_local.reshape(rows_here, B, cols_here, B)
    return blocks4[chosen_row, :, chosen_col, :]


def select_take(received, row_blocks, slots, cols_here):
    mine = lax.axis_index("own") * slots + jnp.arange(slots, dtype=jnp.int32)
    rowlist = row_blocks[mine]
    sender = rowlist // cols_here
    return received[sender]


def on_device(
    sigma_anc, row_blocks, panel1, diag_inv1, mask1, parent_block2, panel2, diag_inv2, mask2
):
    slots = panel1.shape[0]
    cols_here = sigma_anc.shape[1] // B
    keep_own2 = mask2.astype(jnp.float32)
    up_parent = product("kij,kjc->kic", parent_block2, diag_inv2)
    factor2_own = keep_own2[:, :, None] * product("kij,kjc->kic", panel2, diag_inv2)
    factor2_child = shifted(factor2_own, "own", -1)
    outgoing = select_send(sigma_anc, row_blocks, slots)
    received = lax.all_to_all(outgoing, "own", split_axis=0, concat_axis=0, tiled=True)
    blocks1 = select_take(received, row_blocks, slots, cols_here)
    keep1 = mask1.astype(jnp.float32)
    factor1 = keep1[:, :, None] * product("kij,kjc->kic", panel1, diag_inv1)
    factors1 = lax.all_gather(factor1, "row", axis=1, tiled=True).reshape(slots, -1, B, B)
    sel1_panel = -keep1[:, :, None] * product("kmij,kmjc->kic", blocks1, factors1)
    gram1 = product("kji,kjc->kic", diag_inv1, diag_inv1)
    sel1_diag = gram1 - lax.psum(product("kji,kjc->kic", factor1, sel1_panel), "row")
    factor2 = keep1[:, :, None] * factor2_child
    factors2 = lax.all_gather(factor2, "row", axis=1, tiled=True).reshape(slots, -1, B, B)
    anc2 = keep1[:, :, None] * product("kmij,kmjc->kic", blocks1, factors2)
    par_panel = shifted(sel1_panel, "own", 1)
    par_anc = shifted(anc2, "own", 1)
    par_diag = shifted(sel1_diag, "own", 1)
    sel2_panel = -keep_own2[:, :, None] * (product("kij,kjc->kic", par_panel, up_parent) + par_anc)
    cross = product("kji,kjc->kic", par_panel, factor2_own)
    back = product("kji,kjc->kic", factor2_own, sel2_panel)
    par_diag, cross, back = lax.optimization_barrier((par_diag, cross, back))
    cross, back = lax.psum((cross, back), "row")
    sel2_parent = -(product("kij,kjc->kic", par_diag, up_parent) + cross)
    gram2 = product("kji,kjc->kic", diag_inv2, diag_inv2)
    sel2_diag = gram2 - product("kji,kjc->kic", up_parent, sel2_parent) - back
    return (sel1_panel, sel1_diag, sel2_parent, sel2_panel, sel2_diag)


def solution(mesh):
    in_specs = (
        P("row", "own"),
        P(),
        P("own", "row", None),
        P("own", None, None),
        P("own", "row"),
        P("own", None, None),
        P("own", "row", None),
        P("own", None, None),
        P("own", "row"),
    )
    out_specs = (
        P("own", "row", None),
        P("own", None, None),
        P("own", None, None),
        P("own", "row", None),
        P("own", None, None),
    )
    return jax.shard_map(
        on_device, mesh=mesh, in_specs=in_specs, out_specs=out_specs, check_vma=False
    )
```

profile of v0, /device:TPU:2, one launch (start us, length us, event | category | flops | bytes accessed | tf_op | source)
XLA Modules:
  0.0 444.9 jit_solution(6164868798614665549)
XLA Ops:
  7.2 0.0 copy-start
  7.2 0.8 copy.67
  8.0 0.1 constant_dynamic-slice_fusion
  8.1 0.1 copy.90
  8.2 0.1 copy.69
  8.3 0.1 fusion.7
  8.5 0.7 gather_fusion
  9.1 5.9 %reshape.167 = f32[8,256,2,256]{3,2,1,0:T(2,128)} reshape(f32[2048,512]{1,0:T(8,128)} %param.9) | data formatting | bytes 8388608 | tf_op jit(solution)/shard_map/reshape | solution.py:40
  15.1 4.7 %copy.72 = f32[8,256,2,256]{3,1,2,0:T(8,128)} copy(f32[8,256,2,256]{3,2,1,0:T(2,128)} %reshape.167) | data formatting | bytes 8388608 | tf_op jit(solution)/shard_map/reshape | solution.py:40
  19.7 0.2 fusion.11
  19.9 6.5 %gather_fusion.1 = f32[32,256,256]{2,1,0:T(8,128)} fusion(f32[8,256,2,256]{3,1,2,0:T(8,128)} %copy.72, s32[32]{0:T(128)S(1)} %fusion.11), kind=kCustom, calls=%fused_computation.1 | custom fusion | bytes 16777472 | tf_op jit(solution)/shard_map/gather | solution.py:41
  26.5 11.8 %all-to-all-start = ((f32[32,256,256]{2,1,0:T(8,128)}), f32[32,256,256]{2,1,0:T(8,128)}, u32[]{:S(2)}, u32[]{:S(2)}) async-start(f32[32,256,256]{2,1,0:T(8,128)} %gather_fusion.1), calls=%async_computation | async-start | bytes 16777216 | tf_op jit(solution)/shard_map/all_to_all | solution.py:61
  38.3 0.0 all-gather.3.cloned.1.call-start
  38.4 1.5 convolution_multiply_fusion.1
  39.8 0.0 all-gather.3.cloned.1.call-update
  39.8 0.0 all-gather.5.cloned.1.call-start
  39.9 0.7 convolution_multiply_fusion
  40.6 2.8 collective-permute-start.2
  43.3 190.9 %collective-permute-done.2 = f32[2,256,256]{2,1,0:T(8,128)S(1)} collective-permute-done((f32[2,256,256]{2,1,0:T(8,128)S(1)}, f32[2,256,256]{2,1,0:T(8,128)S(1)}, u32[]{:S(2)}, u32[]{:S(2)}) %collective-permute-start.2) | collective-permute-done | bytes 524320 | tf_op jit(solution)/shard_map/ppermute | solution.py:12
  234.2 0.9 broadcast_multiply_fusion
  235.1 0.0 all-gather.5.cloned.1.call-update
  235.1 0.0 all-reduce.4.cloned.1.call-start
  235.2 0.6 gather_fusion.2
  235.8 0.1 reshape.158
  235.9 6.2 %gather_fusion.3 = f32[16,256,256]{2,1,0:T(8,128)} fusion(f32[32,256,256]{2,1,0:T(8,128)} %all-to-all-done, s32[1024]{0:T(1024)S(1)} %pad_clamp_fusion), kind=kCustom, calls=%fused_computation.3 | custom fusion | bytes 8388672 | tf_op jit(solution)/shard_map/gather | solution.py:48
  242.1 8.1 %fusion.3 = f32[2,256,256]{2,1,0:T(8,128)S(1)} fusion(f32[2,8,256,256]{3,2,1,0:T(8,128)} %bitcast.67, f32[2,8,256,256]{3,2,1,0:T(8,128)} %bitcast.69, f32[2]{0:T(128)S(1)} %fusion.16), kind=kOutput, calls=%fused_computation.14 | convolution fusion | flops 3221356544 | bytes 8912904 | tf_op jit(solution)/shard_map/kmij,kmjc->kic/dot_general | solution.py:16
  250.2 0.0 copy-start.3
  250.2 0.3 collective-permute-start.1
  250.5 1.9 fusion.18
  252.4 21.4 %all-gather.5.cloned.1.call-done = f32[2,2048,256]{2,1,0:T(8,128)} async-done(((f32[2,256,256]{2,1,0:T(8,128)}), f32[2,2048,256]{2,1,0:T(8,128)}) %all-gather.5.cloned.1.call-update) | async-done | bytes 4194320 | tf_op jit(solution)/shard_map/all_gather | solution.py:70
  273.8 8.2 %fusion.1 = f32[2,256,256]{2,1,0:T(8,128)} fusion(f32[2,8,256,256]{3,2,1,0:T(8,128)} %bitcast.68, f32[2,8,256,256]{3,2,1,0:T(8,128)} %bitcast.70, f32[2]{0:T(128)S(1)} %convert_bitcast_fusion.1), kind=kOutput, calls=%fused_computation.8 | convolution fusion | flops 3221356544 | bytes 8912904 | tf_op jit(solution)/shard_map/kmij,kmjc->kic/dot_general | solution.py:16
  282.0 1.5 collective-permute-start.3
  283.6 0.0 all-reduce.4.cloned.1.call-update
  283.6 0.0 all-reduce.6.cloned.1.call-start
  283.7 1.7 fusion.20
  285.4 63.5 %all-reduce.4.cloned.1.call-done = f32[2,256,256]{2,1,0:T(8,128)} async-done(((f32[2,256,256]{2,1,0:T(8,128)}), f32[2,256,256]{2,1,0:T(8,128)}) %all-reduce.4.cloned.1.call-update) | async-done | bytes 524304 | tf_op jit(solution)/shard_map/psum | solution.py:68
  348.9 2.9 convolution_subtract_fusion.1
  351.8 1.6 collective-permute-start
  353.3 1.7 fusion.2
  355.0 1.8 fusion.21
  356.9 1.8 fusion.19
  358.7 7.1 %collective-permute-done = f32[2,256,256]{2,1,0:T(8,128)} collective-permute-done((f32[2,256,256]{2,1,0:T(8,128)}, f32[2,256,256]{2,1,0:T(8,128)}, u32[]{:S(2)}, u32[]{:S(2)}) %collective-permute-start) | collective-permute-done | bytes 524320 | tf_op jit(solution)/shard_map/ppermute | solution.py:12
  365.8 0.0 all-reduce.6.cloned.1.call-update
  365.8 1.1 fusion.22
  366.9 67.6 %all-reduce.6.cloned.1.call-done = (f32[2,256,256]{2,1,0:T(8,128)}, f32[2,256,256]{2,1,0:T(8,128)}) async-done(((f32[2,256,256]{2,1,0:T(8,128)}, f32[2,256,256]{2,1,0:T(8,128)}), (f32[2,256,256]{2,1,0:T(8,128)}, f32[2,256,256]{2,1,0:T(8,128)})) %all-reduce.6.cloned.1.call-update) | async-done | bytes 1048592 | tf_op jit(solution)/shard_map/psum | solution.py:79
  434.5 1.9 fusion
  436.4 1.0 convolution_subtract_fusion
  437.5 0.9 sub.48
  (33 shorter events, 0.1 us)
Async XLA Ops:
  7.2 32.7 %copy-start = (f32[2,256,256]{2,1,0:T(8,128)S(1)}, f32[2,256,256]{2,1,0:T(8,128)}, u32[]{:S(2)}) copy-start(f32[2,256,256]{2,1,0:T(8,128)} %param.16) | copy-start | bytes 1572868
  26.4 11.9 %copy-start.9 = (s32[2,1]{0,1:T(1,128)S(1)}, s32[2,1]{0,1:T(1,128)}, u32[]{:S(2)}) copy-start(s32[2,1]{0,1:T(1,128)} %param.13) | copy-start | bytes 28
  26.4 11.9 %copy-start.2 = (f32[2,256,256]{2,1,0:T(8,128)S(1)}, f32[2,256,256]{2,1,0:T(8,128)}, u32[]{:S(2)}) copy-start(f32[2,256,256]{2,1,0:T(8,128)} %param.12) | copy-start | bytes 1572868
  26.4 11.9 %copy-start.7 = (f32[2,256,256]{2,1,0:T(8,128)S(1)}, f32[2,256,256]{2,1,0:T(8,128)}, u32[]{:S(2)}) copy-start(f32[2,256,256]{2,1,0:T(8,128)} %param.11) | copy-start | bytes 1572868
  26.4 13.5 %copy-start.10 = (s32[2,1]{0,1:T(1,128)S(1)}, s32[2,1]{0,1:T(1,128)}, u32[]{:S(2)}) copy-start(s32[2,1]{0,1:T(1,128)} %param.17) | copy-start | bytes 28
  26.4 13.5 %copy-start.8 = (f32[2,256,256]{2,1,0:T(8,128)S(1)}, f32[2,256,256]{2,1,0:T(8,128)}, u32[]{:S(2)}) copy-start(f32[2,256,256]{2,1,0:T(8,128)} %param.15) | copy-start | bytes 1572868
  26.5 209.4 %all-to-all-start = ((f32[32,256,256]{2,1,0:T(8,128)}), f32[32,256,256]{2,1,0:T(8,128)}, u32[]{:S(2)}, u32[]{:S(2)}) async-start(f32[32,256,256]{2,1,0:T(8,128)} %gather_fusion.1), calls=%async_computation | async-start | bytes 16777216 | tf_op jit(solution)/shard_map/all_to_all | solution.py:61
  38.3 203.8 %all-gather.3.cloned.1.call-start = ((), (), s32[]{:S(2)}) async-start(), calls=%async_computation.1 | async-start | bytes 4718592 | tf_op jit(solution)/shard_map/all_gather | solution.py:65
  39.8 234.0 %all-gather.5.cloned.1.call-start = ((), (), s32[]{:S(2)}) async-start(), calls=%async_computation.3 | async-start | bytes 4718592 | tf_op jit(solution)/shard_map/all_gather | solution.py:70
  40.6 193.6 %collective-permute-start.2 = (f32[2,256,256]{2,1,0:T(8,128)S(1)}, f32[2,256,256]{2,1,0:T(8,128)S(1)}, u32[]{:S(2)}, u32[]{:S(2)}) collective-permute-start(f32[2,256,256]{2,1,0:T(8,128)S(1)} %convolution_multiply_fusion), channel_id=1, source_target_pairs={{0,248},{8,0},{16,8},{24,16},{32,24},{40,32},{48,40},{56,48},{64,5... | collective-permute-start | bytes 1572872 | tf_op jit(solution)/shard_map/ppermute | solution.py:12
  235.1 113.7 %all-reduce.4.cloned.1.call-start = ((), (), s32[]{:S(2)}) async-start(), calls=%async_computation.2 | async-start | bytes 1048576 | tf_op jit(solution)/shard_map/psum | solution.py:68
  242.1 8.4 %copy-start.1 = (f32[2,256,256]{2,1,0:T(8,128)S(1)}, f32[2,256,256]{2,1,0:T(8,128)}, u32[]{:S(2)}) copy-start(f32[2,256,256]{2,1,0:T(8,128)} %convolution_multiply_fusion.1) | copy-start | bytes 1572868
  250.2 31.8 %copy-start.3 = (f32[2,256,256]{2,1,0:T(8,128)}, f32[2,256,256]{2,1,0:T(8,128)S(1)}, u32[]{:S(2)}) copy-start(f32[2,256,256]{2,1,0:T(8,128)S(1)} %fusion.3) | copy-start | bytes 1572868
  250.2 103.1 %collective-permute-start.1 = (f32[2,256,256]{2,1,0:T(8,128)S(1)}, f32[2,256,256]{2,1,0:T(8,128)S(1)}, u32[]{:S(2)}, u32[]{:S(2)}) collective-permute-start(f32[2,256,256]{2,1,0:T(8,128)S(1)} %fusion.3), channel_id=1, source_target_pairs={{0,8},{8,16},{16,24},{24,32},{32,40},{40,48},{48,56},{56,64},{64,7... | collective-permute-start | bytes 1572872 | tf_op jit(solution)/shard_map/ppermute | solution.py:12
  282.0 71.3 %collective-permute-start.3 = (f32[2,256,256]{2,1,0:T(8,128)}, f32[2,256,256]{2,1,0:T(8,128)}, u32[]{:S(2)}, u32[]{:S(2)}) collective-permute-start(f32[2,256,256]{2,1,0:T(8,128)} %fusion.1), channel_id=1, source_target_pairs={{0,8},{8,16},{16,24},{24,32},{32,40},{40,48},{48,56},{56,64},{64,7... | collective-permute-start | bytes 1572872 | tf_op jit(solution)/shard_map/ppermute | solution.py:12
  283.6 150.9 %all-reduce.6.cloned.1.call-start = ((), (), s32[]{:S(2)}) async-start(), calls=%async_computation.4 | async-start | bytes 2097152 | tf_op jit(solution)/shard_map/psum | solution.py:79
  351.8 14.1 %collective-permute-start = (f32[2,256,256]{2,1,0:T(8,128)}, f32[2,256,256]{2,1,0:T(8,128)}, u32[]{:S(2)}, u32[]{:S(2)}) collective-permute-start(f32[2,256,256]{2,1,0:T(8,128)} %convolution_subtract_fusion.1), channel_id=1, source_target_pairs={{0,8},{8,16},{16,24},{24,32},{32,40},{40,48},{48,56},{56,64},{64,7... | collective-permute-start | bytes 1572872 | tf_op jit(solution)/shard_map/ppermute | solution.py:12
  355.0 82.5 %copy-start.4 = (f32[2,256,256]{2,1,0:T(8,128)}, f32[2,256,256]{2,1,0:T(8,128)S(1)}, u32[]{:S(2)}) copy-start(f32[2,256,256]{2,1,0:T(8,128)S(1)} %fusion.2) | copy-start | bytes 1572868
  434.5 3.0 copy-start.6
  436.4 2.0 copy-start.5
Sparse Core Ops, SparseCore 0:
  41.5 35.7 all-gather.2
  235.3 38.5 all-gather.4
  283.7 65.0 all-reduce.3
  366.0 68.4 all-reduce.5
where the time goes:
time: 445 us
  waiting for transfers between devices  351 us (79%)
  matrix products  34.3 us (8%)
  local copies, waits for them, and re-layouts  25.7 us (6%)
  starting transfers between devices  18.1 us (4%)
  between operations  14 us (3%)
    ppermute x4, waiting for transfers between devices, shifted(): lax.ppermute(shard, axis, [(i, (i + by) % length) for i in range(length)])  198 us
    psum x1, waiting for transfers between devices, on_device(): cross, back = lax.psum((cross, back), 'row')  67.6 us
    psum x1, waiting for transfers between devices, on_device(): lax.psum(product('kji,kjc->kic', factor1, sel1_panel), 'row')  63.5 us
    dot_general x13, matrix products, product(): return jnp.einsum(form, left, right, precision=HIGH)  34.3 us
    all_gather x1, waiting for transfers between devices, on_device(): lax.all_gather(factor2, 'row', axis=1, tiled=True).reshape(slots, -1, B, B)  21.4 us
    all_to_all x1, starting transfers between devices, on_device(): lax.all_to_all(outgoing, 'own', split_axis=0, concat_axis=0, tiled=True)  11.8 us
    reshape x2, local copies, waits for them, and re-layouts, select_send(): blocks4 = sigma_local.reshape(rows_here, B, cols_here, B)  10.6 us
  transfers between devices with their start and end apart: 9, of which 5 were waited for; matrix products, arithmetic and copies ran while one was open for 9% of the time, Pallas kernels for 0%

commit v1 on v0

--- a/solution.py
+++ b/solution.py
@@ -5,6 +5,27 @@
 
 B = 256
 HIGH = lax.Precision.HIGHEST
+
+
+def gather_around(value, axis, dim):
+    devices, index, rows = (lax.axis_size(axis), lax.axis_index(axis), value.shape[dim])
+    right = [(i, (i + 1) % devices) for i in range(devices)]
+    left = [(i, (i - 1) % devices) for i in range(devices)]
+    out = jnp.zeros((*value.shape[:dim], devices * rows, *value.shape[dim + 1 :]), value.dtype)
+    out = lax.dynamic_update_slice_in_dim(out, value, index * rows, axis=dim)
+    from_left = from_right = value
+    half = devices // 2
+    for turn in range(1, half + 1):
+        from_left = lax.ppermute(from_left, axis, right)
+        out = lax.dynamic_update_slice_in_dim(
+            out, from_left, (index - turn) % devices * rows, axis=dim
+        )
+        if turn < devices - half:
+            from_right = lax.ppermute(from_right, axis, left)
+            out = lax.dynamic_update_slice_in_dim(
+                out, from_right, (index + turn) % devices * rows, axis=dim
+            )
+    return out
 
 
 def shifted(shard, axis, by):
@@ -67,7 +88,7 @@
     gram1 = product("kji,kjc->kic", diag_inv1, diag_inv1)
     sel1_diag = gram1 - lax.psum(product("kji,kjc->kic", factor1, sel1_panel), "row")
     factor2 = keep1[:, :, None] * factor2_child
-    factors2 = lax.all_gather(factor2, "row", axis=1, tiled=True).reshape(slots, -1, B, B)
+    factors2 = gather_around(factor2, "row", 1).reshape(slots, -1, B, B)
     anc2 = keep1[:, :, None] * product("kmij,kmjc->kic", blocks1, factors2)
     par_panel = shifted(sel1_panel, "own", 1)
     par_anc = shifted(anc2, "own", 1)

time: 445 us -> 460 us (1.034)
  local copies, waits for them, and re-layouts: 25.7 us -> 37.4 us
  starting transfers between devices: 18.1 us -> 25.3 us
    all_gather x1 -> x0, waiting for transfers between devices: 21.4 us -> none  [on_device(): lax.all_gather(factor2, 'row', axis=1, tiled=True).reshape(slots, -1, B, B)]
    ppermute x0 -> x7, waiting for transfers between devices: none -> 20.9 us  [the longest x4 20.9 us: gather_around(): from_left = lax.ppermute(from_left, axis, right)]
    dynamic_update_slice x0 -> x7, local copies, waits for them, and re-layouts: none -> 10.1 us  [the longest x4 6.51 us: gather_around(): lax.dynamic_update_slice_in_dim(out, from_left, (index - turn) % devices...]
    ppermute x0 -> x7, starting transfers between devices: none -> 8.89 us  [the longest x3 8.88 us: gather_around(): from_right = lax.ppermute(from_right, axis, left)]
  transfers between devices with their start and end apart: 9 -> 15, of which waited for: 5 -> 8; matrix products, arithmetic and copies ran while one was open for 9% -> 9% of each run, Pallas kernels for 0% -> 0%
where the time goes in v1:
time: 460 us; the launch traced here: 459 us
  waiting for transfers between devices  347 us (75%)
  local copies, waits for them, and re-layouts  37.4 us (8%)
  matrix products  32.2 us (7%)
  starting transfers between devices  25.3 us (6%)
  between operations  14 us (3%)
    ppermute x4, waiting for transfers between devices, shifted(): lax.ppermute(shard, axis, [(i, (i + by) % length) for i in range(length)])  198 us
    psum x1, waiting for transfers between devices, on_device(): cross, back = lax.psum((cross, back), 'row')  67.6 us
    psum x1, waiting for transfers between devices, on_device(): lax.psum(product('kji,kjc->kic', factor1, sel1_panel), 'row')  60.5 us
    dot_general x13, matrix products, product(): return jnp.einsum(form, left, right, precision=HIGH)  32.2 us
    ppermute x4, waiting for transfers between devices, gather_around(): from_left = lax.ppermute(from_left, axis, right)  20.9 us
    all_to_all x1, starting transfers between devices, on_device(): lax.all_to_all(outgoing, 'own', split_axis=0, concat_axis=0, tiled=True)  11.8 us
    reshape x2, local copies, waits for them, and re-layouts, select_send(): blocks4 = sigma_local.reshape(rows_here, B, cols_here, B)  10.6 us
  transfers between devices with their start and end apart: 15, of which 8 were waited for; matrix products, arithmetic and copies ran while one was open for 9% of the time, Pallas kernels for 0%

profile of v1, /device:TPU:2, one launch (start us, length us, event | category | flops | bytes accessed | tf_op | source)
XLA Modules:
  0.0 459.5 jit_solution(8806912630416945596)
XLA Ops:
  7.2 6.0 %reshape.167 = f32[8,256,2,256]{3,2,1,0:T(2,128)} reshape(f32[2048,512]{1,0:T(8,128)} %param.9) | data formatting | bytes 8388608 | tf_op jit(solution)/shard_map/reshape | solution.py:61
  13.2 4.6 %copy.72 = f32[8,256,2,256]{3,1,2,0:T(8,128)} copy(f32[8,256,2,256]{3,2,1,0:T(2,128)} %reshape.167) | data formatting | bytes 8388608 | tf_op jit(solution)/shard_map/reshape | solution.py:61
  17.9 0.1 constant_dynamic-slice_fusion
  18.2 0.1 fusion.6
  18.4 0.7 gather_fusion
  19.0 0.2 fusion.10
  19.2 6.5 %gather_fusion.1 = f32[32,256,256]{2,1,0:T(8,128)} fusion(f32[8,256,2,256]{3,1,2,0:T(8,128)} %copy.72, s32[32]{0:T(128)S(1)} %fusion.10), kind=kCustom, calls=%fused_computation.1 | custom fusion | bytes 16777472 | tf_op jit(solution)/shard_map/gather | solution.py:62
  25.7 11.8 %all-to-all-start = ((f32[32,256,256]{2,1,0:T(8,128)}), f32[32,256,256]{2,1,0:T(8,128)}, u32[]{:S(2)}, u32[]{:S(2)}) async-start(f32[32,256,256]{2,1,0:T(8,128)} %gather_fusion.1), calls=%async_computation | async-start | bytes 16777216 | tf_op jit(solution)/shard_map/all_to_all | solution.py:82
  37.7 1.5 convolution_multiply_fusion.1
  39.2 0.7 convolution_multiply_fusion
  39.9 2.7 collective-permute-start.2
  42.6 190.9 %collective-permute-done.2 = f32[2,256,256]{2,1,0:T(8,128)S(1)} collective-permute-done((f32[2,256,256]{2,1,0:T(8,128)S(1)}, f32[2,256,256]{2,1,0:T(8,128)S(1)}, u32[]{:S(2)}, u32[]{:S(2)}) %collective-permute-start.2) | collective-permute-done | bytes 524320 | tf_op jit(solution)/shard_map/ppermute | solution.py:33
  233.5 2.3 broadcast_in_dim.5
  235.8 1.1 constant_dynamic-update-slice_fusion.6
  236.9 3.0 collective-permute-start.4
  239.9 7.2 %collective-permute-done.3 = f32[2,256,256]{2,1,0:T(8,128)} collective-permute-done((f32[2,256,256]{2,1,0:T(8,128)}, f32[2,256,256]{2,1,0:T(8,128)}, u32[]{:S(2)}, u32[]{:S(2)}) %collective-permute-start.3) | collective-permute-done | bytes 524320 | tf_op jit(solution)/shard_map/ppermute | solution.py:19
  247.0 0.6 gather_fusion.2
  247.6 3.0 collective-permute-start.6
  250.6 6.6 %collective-permute-done.5 = f32[2,256,256]{2,1,0:T(8,128)} collective-permute-done((f32[2,256,256]{2,1,0:T(8,128)}, f32[2,256,256]{2,1,0:T(8,128)}, u32[]{:S(2)}, u32[]{:S(2)}) %collective-permute-start.5) | collective-permute-done | bytes 524320 | tf_op jit(solution)/shard_map/ppermute | solution.py:19
  257.3 0.7 fusion.19
  257.9 3.0 collective-permute-start.8
  260.9 1.9 constant_dynamic-update-slice_fusion.5
  262.8 4.5 collective-permute-done.7
  267.3 0.8 constant_dynamic-update-slice_fusion.4
  268.1 1.9 constant_dynamic-update-slice_fusion.3
  270.0 1.9 constant_dynamic-update-slice_fusion.2
  271.9 1.9 constant_dynamic-update-slice_fusion.1
  273.8 0.8 constant_dynamic-update-slice_fusion
  274.6 2.7 collective-permute-done.9
  277.3 0.8 constant_dynamic-update-slice_fusion.7
  278.1 6.2 %gather_fusion.3 = f32[16,256,256]{2,1,0:T(8,128)} fusion(f32[32,256,256]{2,1,0:T(8,128)} %all-to-all-done, s32[1024]{0:T(1024)S(1)} %pad_clamp_fusion), kind=kCustom, calls=%fused_computation.3 | custom fusion | bytes 8388672 | tf_op jit(solution)/shard_map/gather | solution.py:69
  284.3 8.1 %fusion.2 = f32[2,256,256]{2,1,0:T(8,128)S(1)} fusion(f32[2,8,256,256]{3,2,1,0:T(8,128)} %bitcast.67, f32[2,8,256,256]{3,2,1,0:T(8,128)} %bitcast.69, f32[2]{0:T(128)S(1)} %fusion.15), kind=kOutput, calls=%fused_computation.12 | convolution fusion | flops 3221356544 | bytes 8912904 | tf_op jit(solution)/shard_map/kmij,kmjc->kic/dot_general | solution.py:37
  292.5 1.9 fusion.17
  294.4 0.2 all-reduce.6.cloned.1.call-start
  294.6 8.2 %fusion.1 = f32[2,256,256]{2,1,0:T(8,128)} fusion(f32[2,8,256,256]{3,2,1,0:T(8,128)} %bitcast.68, f32[2,8,256,256]{3,2,1,0:T(8,128)} %bitcast.11, f32[2]{0:T(128)S(1)} %convert_bitcast_fusion.1), kind=kOutput, calls=%fused_computation.8 | convolution fusion | flops 3221356544 | bytes 8912904 | tf_op jit(solution)/shard_map/kmij,kmjc->kic/dot_general | solution.py:37
  302.9 60.5 %all-reduce.4.cloned.1.call-done = f32[2,256,256]{2,1,0:T(8,128)} async-done(((f32[2,256,256]{2,1,0:T(8,128)}), f32[2,256,256]{2,1,0:T(8,128)}) %all-reduce.4.cloned.1.call-update) | async-done | bytes 524304 | tf_op jit(solution)/shard_map/psum | solution.py:89
  363.4 2.9 convolution_subtract_fusion.1
  366.3 1.6 collective-permute-start
  367.9 0.7 fusion.20
  368.5 1.1 add_multiply_fusion
  369.7 1.8 fusion.21
  371.5 1.8 fusion.18
  373.4 7.0 %collective-permute-done = f32[2,256,256]{2,1,0:T(8,128)} collective-permute-done((f32[2,256,256]{2,1,0:T(8,128)}, f32[2,256,256]{2,1,0:T(8,128)}, u32[]{:S(2)}, u32[]{:S(2)}) %collective-permute-start) | collective-permute-done | bytes 524320 | tf_op jit(solution)/shard_map/ppermute | solution.py:33
  380.4 1.1 fusion.22
  381.5 67.6 %all-reduce.6.cloned.1.call-done = (f32[2,256,256]{2,1,0:T(8,128)}, f32[2,256,256]{2,1,0:T(8,128)}) async-done(((f32[2,256,256]{2,1,0:T(8,128)}, f32[2,256,256]{2,1,0:T(8,128)}), (f32[2,256,256]{2,1,0:T(8,128)}, f32[2,256,256]{2,1,0:T(8,128)})) %all-reduce.6.cloned.1.call-update) | async-done | bytes 1048592 | tf_op jit(solution)/shard_map/psum | solution.py:100
  449.1 1.9 fusion
  451.0 1.0 convolution_subtract_fusion
  452.1 0.9 sub.64
  (57 shorter events, 0.7 us)
Async XLA Ops:
  7.2 32.0 %copy-start = (f32[2,256,256]{2,1,0:T(8,128)S(1)}, f32[2,256,256]{2,1,0:T(8,128)}, u32[]{:S(2)}) copy-start(f32[2,256,256]{2,1,0:T(8,128)} %param.16) | copy-start | bytes 1572868
  13.2 4.6 %copy-start.10 = (s32[64,8]{0,1:T(8,128)S(1)}, s32[64,8]{0,1:T(8,128)}, u32[]{:S(2)}) copy-start(s32[64,8]{0,1:T(8,128)} %param.10) | copy-start | bytes 6148
  25.7 11.9 %copy-start.11 = (s32[2,1]{0,1:T(1,128)S(1)}, s32[2,1]{0,1:T(1,128)}, u32[]{:S(2)}) copy-start(s32[2,1]{0,1:T(1,128)} %param.13) | copy-start | bytes 28
  25.7 11.9 %copy-start.2 = (f32[2,256,256]{2,1,0:T(8,128)S(1)}, f32[2,256,256]{2,1,0:T(8,128)}, u32[]{:S(2)}) copy-start(f32[2,256,256]{2,1,0:T(8,128)} %param.12) | copy-start | bytes 1572868
  25.7 11.9 %copy-start.8 = (f32[2,256,256]{2,1,0:T(8,128)S(1)}, f32[2,256,256]{2,1,0:T(8,128)}, u32[]{:S(2)}) copy-start(f32[2,256,256]{2,1,0:T(8,128)} %param.11) | copy-start | bytes 1572868
  25.7 13.5 %copy-start.12 = (s32[2,1]{0,1:T(1,128)S(1)}, s32[2,1]{0,1:T(1,128)}, u32[]{:S(2)}) copy-start(s32[2,1]{0,1:T(1,128)} %param.17) | copy-start | bytes 28
  25.7 13.5 %copy-start.9 = (f32[2,256,256]{2,1,0:T(8,128)S(1)}, f32[2,256,256]{2,1,0:T(8,128)}, u32[]{:S(2)}) copy-start(f32[2,256,256]{2,1,0:T(8,128)} %param.15) | copy-start | bytes 1572868
  25.7 252.4 %all-to-all-start = ((f32[32,256,256]{2,1,0:T(8,128)}), f32[32,256,256]{2,1,0:T(8,128)}, u32[]{:S(2)}, u32[]{:S(2)}) async-start(f32[32,256,256]{2,1,0:T(8,128)} %gather_fusion.1), calls=%async_computation | async-start | bytes 16777216 | tf_op jit(solution)/shard_map/all_to_all | solution.py:82
  37.6 246.8 %all-gather.2.cloned.1.call-start = ((), (), s32[]{:S(2)}) async-start(), calls=%async_computation.1 | async-start | bytes 4718592 | tf_op jit(solution)/shard_map/all_gather | solution.py:86
  39.1 218.1 %copy-start.6 = (f32[2,256,256]{2,1,0:T(8,128)S(1)}, f32[2,256,256]{2,1,0:T(8,128)}, u32[]{:S(2)}) copy-start(f32[2,256,256]{2,1,0:T(8,128)} %param.14) | copy-start | bytes 1572868
  39.1 324.3 %all-reduce.4.cloned.1.call-start = ((), (), s32[]{:S(2)}) async-start(), calls=%async_computation.2 | async-start | bytes 1048576 | tf_op jit(solution)/shard_map/psum | solution.py:89
  39.9 193.6 %collective-permute-start.2 = (f32[2,256,256]{2,1,0:T(8,128)S(1)}, f32[2,256,256]{2,1,0:T(8,128)S(1)}, u32[]{:S(2)}, u32[]{:S(2)}) collective-permute-start(f32[2,256,256]{2,1,0:T(8,128)S(1)} %convolution_multiply_fusion), channel_id=1, source_target_pairs={{0,248},{8,0},{16,8},{24,16},{32,24},{40,32},{48,40},{56,48},{64,5... | collective-permute-start | bytes 1572872 | tf_op jit(solution)/shard_map/ppermute | solution.py:33
  236.9 10.1 %collective-permute-start.3 = (f32[2,256,256]{2,1,0:T(8,128)}, f32[2,256,256]{2,1,0:T(8,128)}, u32[]{:S(2)}, u32[]{:S(2)}) collective-permute-start(f32[2,256,256]{2,1,0:T(8,128)} %get-tuple-element.14), channel_id=1, source_target_pairs={{0,1},{1,2},{2,3},{3,4},{4,5},{5,6},{6,7},{7,0},{8,9},{9,10},{10,1... | collective-permute-start | bytes 1572872 | tf_op jit(solution)/shard_map/ppermute | solution.py:19
  236.9 10.7 %collective-permute-start.4 = (f32[2,256,256]{2,1,0:T(8,128)}, f32[2,256,256]{2,1,0:T(8,128)S(1)}, u32[]{:S(2)}, u32[]{:S(2)}) collective-permute-start(f32[2,256,256]{2,1,0:T(8,128)} %get-tuple-element.14), channel_id=1, source_target_pairs={{0,7},{1,0},{2,1},{3,2},{4,3},{5,4},{6,5},{7,6},{8,15},{9,8},{10,9... | collective-permute-start | bytes 1572872 | tf_op jit(solution)/shard_map/ppermute | solution.py:24
  247.0 10.1 %collective-permute-start.5 = (f32[2,256,256]{2,1,0:T(8,128)}, f32[2,256,256]{2,1,0:T(8,128)}, u32[]{:S(2)}, u32[]{:S(2)}) collective-permute-start(f32[2,256,256]{2,1,0:T(8,128)} %collective-permute-done.3), channel_id=1, source_target_pairs={{0,1},{1,2},{2,3},{3,4},{4,5},{5,6},{6,7},{7,0},{8,9},{9,10},{10,1... | collective-permute-start | bytes 1572872 | tf_op jit(solution)/shard_map/ppermute | solution.py:19
  247.6 10.3 %collective-permute-start.6 = (f32[2,256,256]{2,1,0:T(8,128)S(1)}, f32[2,256,256]{2,1,0:T(8,128)}, u32[]{:S(2)}, u32[]{:S(2)}) collective-permute-start(f32[2,256,256]{2,1,0:T(8,128)S(1)} %collective-permute-done.4), channel_id=1, source_target_pairs={{0,7},{1,0},{2,1},{3,2},{4,3},{5,4},{6,5},{7,6},{8,15},{9,8},{10,9... | collective-permute-start | bytes 1572872 | tf_op jit(solution)/shard_map/ppermute | solution.py:24
  257.2 10.1 %collective-permute-start.7 = (f32[2,256,256]{2,1,0:T(8,128)}, f32[2,256,256]{2,1,0:T(8,128)}, u32[]{:S(2)}, u32[]{:S(2)}) collective-permute-start(f32[2,256,256]{2,1,0:T(8,128)} %collective-permute-done.5), channel_id=1, source_target_pairs={{0,1},{1,2},{2,3},{3,4},{4,5},{5,6},{6,7},{7,0},{8,9},{9,10},{10,1... | collective-permute-start | bytes 1572872 | tf_op jit(solution)/shard_map/ppermute | solution.py:19
  257.9 15.9 %collective-permute-start.8 = (f32[2,256,256]{2,1,0:T(8,128)}, f32[2,256,256]{2,1,0:T(8,128)S(1)}, u32[]{:S(2)}, u32[]{:S(2)}) collective-permute-start(f32[2,256,256]{2,1,0:T(8,128)} %collective-permute-done.6), channel_id=1, source_target_pairs={{0,7},{1,0},{2,1},{3,2},{4,3},{5,4},{6,5},{7,6},{8,15},{9,8},{10,9... | collective-permute-start | bytes 1572872 | tf_op jit(solution)/shard_map/ppermute | solution.py:24
  267.3 10.0 %collective-permute-start.9 = (f32[2,256,256]{2,1,0:T(8,128)}, f32[2,256,256]{2,1,0:T(8,128)S(1)}, u32[]{:S(2)}, u32[]{:S(2)}) collective-permute-start(f32[2,256,256]{2,1,0:T(8,128)} %collective-permute-done.7), channel_id=1, source_target_pairs={{0,1},{1,2},{2,3},{3,4},{4,5},{5,6},{6,7},{7,0},{8,9},{9,10},{10,1... | collective-permute-start | bytes 1572872 | tf_op jit(solution)/shard_map/ppermute | solution.py:19
  284.3 8.1 %copy-start.1 = (f32[2,256,256]{2,1,0:T(8,128)S(1)}, f32[2,256,256]{2,1,0:T(8,128)}, u32[]{:S(2)}) copy-start(f32[2,256,256]{2,1,0:T(8,128)} %convolution_multiply_fusion.1) | copy-start | bytes 1572868
  292.5 10.4 %copy-start.3 = (f32[2,256,256]{2,1,0:T(8,128)}, f32[2,256,256]{2,1,0:T(8,128)S(1)}, u32[]{:S(2)}) copy-start(f32[2,256,256]{2,1,0:T(8,128)S(1)} %fusion.2) | copy-start | bytes 1572868
  294.4 73.5 %collective-permute-start.1 = (f32[2,256,256]{2,1,0:T(8,128)S(1)}, f32[2,256,256]{2,1,0:T(8,128)S(1)}, u32[]{:S(2)}, u32[]{:S(2)}) collective-permute-start(f32[2,256,256]{2,1,0:T(8,128)S(1)} %fusion.2), channel_id=1, source_target_pairs={{0,8},{8,16},{16,24},{24,32},{32,40},{40,48},{48,56},{56,64},{64,7... | collective-permute-start | bytes 1572872 | tf_op jit(solution)/shard_map/ppermute | solution.py:33
  294.4 154.7 %all-reduce.6.cloned.1.call-start = ((), (), s32[]{:S(2)}) async-start(), calls=%async_computation.3 | async-start | bytes 2097152 | tf_op jit(solution)/shard_map/psum | solution.py:100
  302.9 65.7 %collective-permute-start.10 = (f32[2,256,256]{2,1,0:T(8,128)}, f32[2,256,256]{2,1,0:T(8,128)}, u32[]{:S(2)}, u32[]{:S(2)}) collective-permute-start(f32[2,256,256]{2,1,0:T(8,128)} %fusion.1), channel_id=1, source_target_pairs={{0,8},{8,16},{16,24},{24,32},{32,40},{40,48},{48,56},{56,64},{64,7... | collective-permute-start | bytes 1572872 | tf_op jit(solution)/shard_map/ppermute | solution.py:33
  366.3 14.1 %collective-permute-start = (f32[2,256,256]{2,1,0:T(8,128)}, f32[2,256,256]{2,1,0:T(8,128)}, u32[]{:S(2)}, u32[]{:S(2)}) collective-permute-start(f32[2,256,256]{2,1,0:T(8,128)} %convolution_subtract_fusion.1), channel_id=1, source_target_pairs={{0,8},{8,16},{16,24},{24,32},{32,40},{40,48},{48,56},{56,64},{64,7... | collective-permute-start | bytes 1572872 | tf_op jit(solution)/shard_map/ppermute | solution.py:33
  369.7 82.4 %copy-start.4 = (f32[2,256,256]{2,1,0:T(8,128)}, f32[2,256,256]{2,1,0:T(8,128)S(1)}, u32[]{:S(2)}) copy-start(f32[2,256,256]{2,1,0:T(8,128)S(1)} %add_multiply_fusion) | copy-start | bytes 1572868
  449.1 3.0 copy-start.7
  451.0 2.0 copy-start.5
Sparse Core Ops, SparseCore 0:
  40.8 35.7 all-gather.1
  294.5 68.8 all-reduce.3
  380.5 68.4 all-reduce.5
